TPU v7x, 128 devices: a whole 4x4x4 slice. The times are simulated.
128 devices in a mesh: az: 16 (over x_hi, z, core), tm: 8 (over x_lo, y).
Axes of the slice: x: 4 (x_hi: 2, x_lo: 2; x = x_hi * 2 + x_lo), y: 4, z: 4, core: 2. Of those that a mesh axis runs over, the one named last changes fastest.
Arguments:
- pressure: bfloat16 [16, 64, 128, 4096], P(None, 'az', 'tm'), may hold values from -6 to 6
- offsets: int32 [128, 16], P('tm'), may hold values from -1 to 0
- frac: float32 [128, 16], P('tm'), may hold values from 0 to 1
Outputs:
- csm: float32 [256, 2, 1024, 1024], P('tm', None, 'az')
All inputs are finite; a program needn't handle non-finite values.
Results may differ from a plain program's by a relative error of at most 0.0065.
Values may be sent and summed in bfloat16 or wider, within the bound.
No kernel may reach another device: no remote copies, remote signals or barrier semaphores. Data moves between devices by JAX's collectives and lax.ppermute only.
A program may use at most 192 MiB of HBM per device.

v0:
```python
import math
import jax
import jax.numpy as jnp
from jax import lax
from jax.sharding import PartitionSpec as P

FREQS = 256


def extended(block, sides, width):
    for axis, dim in sides:
        count = lax.axis_size(axis)
        forward = [(i, i + 1) for i in range(count - 1)]
        forward.append((count - 1, 0))
        backward = [(target, source) for source, target in forward]
        low = lax.ppermute(
            lax.slice_in_dim(block, block.shape[dim] - width, None, axis=dim), axis, forward
        )
        high = lax.ppermute(lax.slice_in_dim(block, 0, width, axis=dim), axis, backward)
        block = jnp.concatenate([low, block, high], axis=dim)
    return block


def dft_table(length, freqs):
    times = jnp.arange(length, dtype=jnp.int32)
    bins = jnp.arange(1, freqs + 1, dtype=jnp.int32)
    phase = (times[:, None] * bins[None, :] % length).astype(jnp.float32) * (2.0 * math.pi / length)
    hann = 0.5 - 0.5 * jnp.cos(times.astype(jnp.float32) * (2.0 * math.pi / length))
    factor = hann[:, None] / math.sqrt(3.0 * length / 8.0)
    return jnp.concatenate([factor * jnp.cos(phase), -factor * jnp.sin(phase)], axis=1).astype(
        jnp.bfloat16
    )


def interp_weights(offsets, frac):
    rows = []
    for shift in range(-1, 2):
        low = (offsets == shift).astype(frac.dtype)
        high = (offsets + 1 == shift).astype(frac.dtype)
        rows.append((1.0 - frac) * low + frac * high)
    return jnp.stack(rows, 0)


def rotated_rows(rows):
    split = rows.reshape(rows.shape[0], rows.shape[1], rows.shape[2] // 2, 2)
    return jnp.stack([split[..., 1], -split[..., 0]], -1).reshape(rows.shape)


def cross_terms(rows, turned, columns):
    real = jnp.einsum("fqk,fpk->fqp", rows, columns, preferred_element_type=jnp.float32)
    imag = jnp.einsum("fqk,fpk->fqp", turned, columns, preferred_element_type=jnp.float32)
    return jnp.stack([real, imag], 1)


def shards(pressure, offsets, frac):
    cycles, sector, blocks, length = pressure.shape
    subs = offsets.shape[1]
    sub_len = length // subs
    padded = extended(pressure, (("az", 1),), 1)
    weights = interp_weights(offsets, frac)
    total = jnp.zeros((cycles, sector, blocks, subs, sub_len), jnp.float32)
    for shift in range(3):
        moved = padded[:, shift : shift + sector].reshape(cycles, sector, blocks, subs, sub_len)
        total = total + weights[shift][None, None, :, :, None] * moved
    virtual = total.astype(jnp.bfloat16).reshape(cycles * sector * blocks, length)
    table = dft_table(length, FREQS)
    freqs = table.shape[1] // 2
    spectra = jnp.dot(virtual, table, preferred_element_type=jnp.float32).astype(jnp.bfloat16)
    spectra = spectra.reshape(cycles, sector, blocks, 2, freqs).transpose(4, 1, 0, 2, 3)
    spectra = spectra.reshape(freqs, sector * cycles, blocks, 2)
    local_rows = sector * cycles
    gathered = lax.all_gather(spectra, "az", axis=1, tiled=True)
    shared = lax.all_to_all(gathered, "tm", split_axis=0, concat_axis=2, tiled=True)
    width = shared.shape[2]
    columns = shared.reshape(shared.shape[0], shared.shape[1], width * 2)
    start = lax.axis_index("az") * local_rows
    rows = lax.dynamic_slice_in_dim(columns, start, local_rows, 1)
    result = cross_terms(rows, rotated_rows(rows), columns)
    return result * (1.0 / width)


def solution(mesh):
    return jax.shard_map(
        shards,
        mesh=mesh,
        in_specs=(P(None, "az", "tm", None), P("tm", None), P("tm", None)),
        out_specs=P("tm", None, "az", None),
        check_vma=False,
    )
```

profile of v0, /device:TPU:1, one launch (start us, length us, event | category | flops | bytes accessed | tf_op | source)
XLA Modules:
  0.0 562.0 jit_solution(8039521140243428556)
XLA Ops:
  6.5 0.0 copy-start
  6.5 0.0 copy-start.1
  6.5 0.0 all-gather.2.cloned.1.call-start
  6.5 4.7 fusion.19
  11.3 3.0 collective-permute-start
  14.3 0.0 collective-permute-start.1
  14.3 0.0 copy-done
  14.3 0.0 copy-done.1
  14.3 2.1 mul.142
  16.5 19.6 %copy.35 = f32[128,8,16,256]{3,1,2,0:T(8,128)} copy(f32[128,8,16,256]{3,2,1,0:T(8,128)S(1)} %bitcast.38) | data formatting | bytes 33554432
  36.1 2.1 mul.137
  38.2 19.0 %copy.34 = f32[128,8,16,256]{3,1,2,0:T(8,128)} copy(f32[128,8,16,256]{3,2,1,0:T(8,128)S(1)} %bitcast.39) | data formatting | bytes 33554432
  57.3 2.1 mul.132
  59.4 0.0 slice-start
  59.4 0.0 slice-start.1
  59.4 19.3 %copy.33 = f32[128,8,16,256]{3,1,2,0:T(8,128)} copy(f32[128,8,16,256]{3,2,1,0:T(8,128)S(1)} %bitcast.40) | data formatting | bytes 33554432
  78.8 0.1 subtract_multiply_fusion
  78.8 0.0 slice-start.2
  78.8 19.2 %multiply_convert_fusion.1 = (bf16[4096,256]{1,0:T(8,128)(2,1)}, bf16[4096,256]{1,0:T(8,128)(2,1)}) fusion(s32[256]{0:T(256)S(1)} %iota_add_fusion, f32[4096]{0:T(1024)S(1)} %get-tuple-element.16, f32[4096]{0:T(1024)S(1)} %get-tuple-element.17), kind=kLoop, calls=%fused_computation.20 | loop fusion | flops 18874368 | bytes 4228096 | tf_op jit(solution)/shard_map/convert.3
  98.0 0.0 slice-start.3
  98.0 0.0 collective-permute-done
  98.0 0.0 collective-permute-done.1
  98.1 0.0 slice-done
  98.1 0.0 slice-done.1
  98.1 8.1 %pad_maximum_fusion.1 = (bf16[16,4,16,4096]{3,2,1,0:T(8,128)(2,1)}, bf16[16,4,16,4096]{3,2,1,0:T(8,128)(2,1)}) fusion(bf16[16,4,16,4096]{3,2,1,0:T(8,128)(2,1)S(1)} %bitcast.43, bf16[16,1,16,4096]{3,2,1,0:T(8,128)(2,1)} %collective-permute-done, bf16[16,1,16,4096]{3,2,1,0:T(8,128)(2,1)} %collective-permute-done.1), kind=kLoop, calls=%fused_computation.8 | loop fusion | flops 8388608 | bytes 29360128 | tf_op jit(solution)/shard_map/concatenate | solution.py:20
  106.1 0.0 slice-done.2
  106.2 0.0 slice-done.3
  106.2 26.0 %fusion.1 = bf16[1024,4096]{1,0:T(8,128)(2,1)} fusion(f32[1024,4096]{1,0:T(8,128)} %bitcast.35, f32[1024,4096]{1,0:T(8,128)} %bitcast.36, f32[1024,4096]{1,0:T(8,128)} %bitcast.37, bf16[16,4,16,4096]{3,2,1,0:T(8,128)(2,1)} %get-tuple-element.6, bf16[16,4,16,4096]{3,2,1,0:T(8,128)(2,1)S(1)} %bitcast.45, bf16[16,4,16,4096]{3,2,1,0:T(8,128)(2,1)} %get-tuple-element.5), kind=kLoop, calls=%fused_computation.3 | loop fusion | flops 37748736 | bytes 83886080 | tf_op jit(solution)/shard_map/convert_element_type | solution.py:65
  132.2 9.1 %fusion.14 = bf16[1024,512]{1,0:T(8,128)(2,1)S(1)} fusion(bf16[1024,4096]{1,0:T(8,128)(2,1)} %fusion.1, bf16[4096,256]{1,0:T(8,128)(2,1)} %get-tuple-element.15, bf16[4096,256]{1,0:T(8,128)(2,1)} %get-tuple-element.14), kind=kOutput, calls=%fused_computation.28 | convolution fusion | flops 4303880192 | bytes 13631488 | tf_op jit(solution)/shard_map/dot_general | solution.py:68
  141.2 0.5 reshape.53
  141.7 1.2 copy.24
  142.9 0.0 all-gather.2.cloned.1.call-update
  142.9 111.5 %all-gather.2.cloned.1.call-done = bf16[256,1024,16,2]{0,2,3,1:T(8,128)(2,1)} async-done(((bf16[256,64,16,2]{0,2,3,1:T(8,128)(2,1)}), bf16[256,1024,16,2]{0,2,3,1:T(8,128)(2,1)}) %all-gather.2.cloned.1.call-update) | async-done | bytes 16777232 | tf_op jit(solution)/shard_map/all_gather | solution.py:72
  254.4 26.0 %copy.25 = bf16[256,1024,16,2]{1,2,3,0:T(8,128)(2,1)} copy(bf16[256,1024,16,2]{0,2,3,1:T(8,128)(2,1)} %all-gather.2.cloned.1.call-done) | data formatting | bytes 33554432 | tf_op jit(solution)/shard_map/all_gather | solution.py:72
  280.4 5.7 %all-to-all-start = ((bf16[256,1024,16,2]{1,2,3,0:T(8,128)(2,1)}), bf16[256,1024,16,2]{1,2,3,0:T(8,128)(2,1)}, u32[]{:S(2)}, u32[]{:S(2)}) async-start(bf16[256,1024,16,2]{1,2,3,0:T(8,128)(2,1)} %copy.25), calls=%async_computation | async-start | bytes 33554432 | tf_op jit(solution)/shard_map/all_to_all | solution.py:73
  286.1 183.5 %all-to-all-done = bf16[256,1024,16,2]{1,2,3,0:T(8,128)(2,1)} async-done(((bf16[256,1024,16,2]{1,2,3,0:T(8,128)(2,1)}), bf16[256,1024,16,2]{1,2,3,0:T(8,128)(2,1)}, u32[]{:S(2)}, u32[]{:S(2)}) %all-to-all-start) | async-done | bytes 16777248 | tf_op jit(solution)/shard_map/all_to_all | solution.py:73
  469.6 18.6 %copy.26 = bf16[32,1024,8,16,2]{1,0,4,3,2:T(8,128)(2,1)} copy(bf16[32,1024,8,16,2]{1,3,4,0,2:T(8,128)(2,1)} %bitcast.6) | data formatting | bytes 33554432 | tf_op jit(solution)/shard_map/all_to_all | solution.py:73
  488.3 23.2 %copy.27 = bf16[32,1024,256]{2,1,0:T(8,128)(2,1)} copy(bf16[32,1024,256]{1,0,2:T(8,128)(2,1)} %bitcast.41) | data formatting | bytes 33554432 | tf_op jit(solution)/shard_map/reshape | solution.py:75
  511.5 1.3 constant_dynamic-slice_fusion
  512.8 3.1 copy.29
  515.9 14.2 %convolution_bitcast_fusion = f32[32,1,64,1024]{3,2,0,1:T(8,128)} fusion(bf16[32,64,256]{2,1,0:T(8,128)(2,1)S(1)} %constant_dynamic-slice_fusion, bf16[32,1024,256]{2,1,0:T(8,128)(2,1)} %copy.27), kind=kOutput, calls=%fused_computation.24 | convolution fusion | flops 1073741824 | bytes 26214400 | tf_op jit(solution)/shard_map/fqk,fpk->fqp/dot_general | solution.py:50
  530.0 0.2 fusion.20
  530.2 0.4 pad_maximum_fusion.2
  530.6 11.2 %convolution_bitcast_fusion.1 = f32[32,1,64,1024]{3,2,0,1:T(8,128)} fusion(bf16[32,1024,256]{2,1,0:T(8,128)(2,1)} %copy.27, bf16[32,64,256]{1,0,2:T(8,128)(2,1)S(1)} %bitcast.46), kind=kOutput, calls=%fused_computation.25 | convolution fusion | flops 1073741824 | bytes 26214400 | tf_op jit(solution)/shard_map/fqk,fpk->fqp/dot_general | solution.py:51
  541.9 6.8 %maximum_multiply_fusion = f32[32,2,64,1024]{3,2,0,1:T(8,128)S(1)} fusion(f32[32,1,64,1024]{3,2,0,1:T(8,128)} %convolution_bitcast_fusion.1, f32[32,1,64,1024]{3,2,0,1:T(8,128)} %convolution_bitcast_fusion), kind=kLoop, calls=%fused_computation | loop fusion | flops 8388608 | bytes 33554432 | tf_op jit(solution)/shard_map/mul | solution.py:79
  548.7 6.2 %copy.32 = f32[32,2,64,1024]{3,2,1,0:T(8,128)} copy(f32[32,2,64,1024]{3,2,0,1:T(8,128)S(1)} %maximum_multiply_fusion) | data formatting | bytes 33554432 | tf_op jit(solution)/shard_map/mul | solution.py:79
  (4 shorter events, 0.0 us)
Async XLA Ops:
  6.5 7.8 %copy-start = (f32[16,16]{1,0:T(8,128)S(1)}, f32[16,16]{1,0:T(8,128)}, u32[]{:S(2)}) copy-start(f32[16,16]{1,0:T(8,128)} %param.5) | copy-start | bytes 3076
  6.5 7.8 %copy-start.1 = (s32[16,16]{1,0:T(8,128)S(1)}, s32[16,16]{1,0:T(8,128)}, u32[]{:S(2)}) copy-start(s32[16,16]{1,0:T(8,128)} %param.4) | copy-start | bytes 3076
  6.5 247.9 %all-gather.2.cloned.1.call-start = ((), (), s32[]{:S(2)}) async-start(), calls=%async_computation.1 | async-start | bytes 17825792 | tf_op jit(solution)/shard_map/all_gather | solution.py:72
  11.3 86.8 %collective-permute-start = (bf16[16,1,16,4096]{3,2,1,0:T(8,128)(2,1)}, bf16[16,1,16,4096]{3,2,1,0:T(8,128)(2,1)}, u32[]{:S(2)}, u32[]{:S(2)}) collective-permute-start(bf16[16,1,16,4096]{3,2,1,0:T(8,128)(2,1)} %get-tuple-element.7), channel_id=1, source_target_pairs={{0,8},{8,16},{16,24},{24,32},{32,40},{40,48},{48,56},{56,64},{64,7... | collective-permute-start | bytes 6291464 | tf_op jit(solution)/shard_map/ppermute | solution.py:16
  14.3 83.8 %collective-permute-start.1 = (bf16[16,1,16,4096]{3,2,1,0:T(8,128)(2,1)}, bf16[16,1,16,4096]{3,2,1,0:T(8,128)(2,1)}, u32[]{:S(2)}, u32[]{:S(2)}) collective-permute-start(bf16[16,1,16,4096]{3,2,1,0:T(8,128)(2,1)} %get-tuple-element.8), channel_id=1, source_target_pairs={{8,0},{16,8},{24,16},{32,24},{40,32},{48,40},{56,48},{64,56},{72,6... | collective-permute-start | bytes 6291464 | tf_op jit(solution)/shard_map/ppermute | solution.py:19
  59.4 38.7 %slice-start = ((s8[8388608]{0:T(1024)(128)(4,1)}), s8[4194304]{0:T(1024)(128)(4,1)S(1)}, s32[]{:S(2)}) async-start(s8[8388608]{0:T(1024)(128)(4,1)} %bitcast.42), calls=%async_computation.2 | async-start | bytes 8388608
  59.4 38.6 %slice-start.1 = ((s8[8388608]{0:T(1024)(128)(4,1)}), s8[4194304]{0:T(1024)(128)(4,1)S(1)}, s32[]{:S(2)}) async-start(s8[8388608]{0:T(1024)(128)(4,1)} %bitcast.42), calls=%async_computation.3 | async-start | bytes 8388608
  78.8 27.3 %slice-start.2 = ((s8[8388608]{0:T(1024)(128)(4,1)}), s8[4194304]{0:T(1024)(128)(4,1)S(1)}, s32[]{:S(2)}) async-start(s8[8388608]{0:T(1024)(128)(4,1)} %bitcast.44), calls=%async_computation.4 | async-start | bytes 8388608
  98.0 8.1 %slice-start.3 = ((s8[8388608]{0:T(1024)(128)(4,1)}), s8[4194304]{0:T(1024)(128)(4,1)S(1)}, s32[]{:S(2)}) async-start(s8[8388608]{0:T(1024)(128)(4,1)} %bitcast.44), calls=%async_computation.5 | async-start | bytes 8388608
  280.4 189.2 %all-to-all-start = ((bf16[256,1024,16,2]{1,2,3,0:T(8,128)(2,1)}), bf16[256,1024,16,2]{1,2,3,0:T(8,128)(2,1)}, u32[]{:S(2)}, u32[]{:S(2)}) async-start(bf16[256,1024,16,2]{1,2,3,0:T(8,128)(2,1)} %copy.25), calls=%async_computation | async-start | bytes 33554432 | tf_op jit(solution)/shard_map/all_to_all | solution.py:73
Sparse Core Ops, SparseCore 0:
  143.1 111.2 all-gather.1
where the time goes:
time: 566 us; the launch traced here: 562 us
  waiting for transfers between devices  295 us (52%)
  local copies, waits for them, and re-layouts  149 us (26%)
  other arithmetic  60.8 us (11%)
  matrix products  34.5 us (6%)
  between operations  13.8 us (2%)
  starting transfers between devices  8.76 us (2%)
    all_to_all x1, waiting for transfers between devices, shards(): lax.all_to_all(gathered, 'tm', split_axis=0, concat_axis=2, tiled=True)  183 us
    all_gather x1, waiting for transfers between devices, shards(): gathered = lax.all_gather(spectra, 'az', axis=1, tiled=True)  111 us
    unnamed x15, local copies, waits for them, and re-layouts  58 us
    convert_element_type x1, other arithmetic, shards(): total.astype(jnp.bfloat16).reshape(cycles * sector * blocks, length)  26 us
    all_gather x1, local copies, waits for them, and re-layouts, shards(): gathered = lax.all_gather(spectra, 'az', axis=1, tiled=True)  26 us
    reshape x1, local copies, waits for them, and re-layouts, shards(): columns = shared.reshape(shared.shape[0], shared.shape[1], width * 2)  23.2 us
    another operation x1, other arithmetic  19.2 us
    all_to_all x1, local copies, waits for them, and re-layouts, shards(): lax.all_to_all(gathered, 'tm', split_axis=0, concat_axis=2, tiled=True)  18.6 us
  transfers between devices with their start and end apart: 4, of which 2 were waited for; matrix products, arithmetic and copies ran while one was open for 15% of the time, Pallas kernels for 0%

commit v1 on v0

--- a/solution.py
+++ b/solution.py
@@ -5,6 +5,9 @@
 from jax.sharding import PartitionSpec as P
 
 FREQS = 256
+_rest_slabs = lambda packet, shard_axis: jnp.concatenate(
+    lax.all_to_all(jnp.stack([packet] * lax.axis_size(shard_axis), 0), shard_axis, 0, 0), axis=1
+)
 
 
 def extended(block, sides, width):
@@ -69,7 +72,7 @@
     spectra = spectra.reshape(cycles, sector, blocks, 2, freqs).transpose(4, 1, 0, 2, 3)
     spectra = spectra.reshape(freqs, sector * cycles, blocks, 2)
     local_rows = sector * cycles
-    gathered = lax.all_gather(spectra, "az", axis=1, tiled=True)
+    gathered = _rest_slabs(spectra, "az")
     shared = lax.all_to_all(gathered, "tm", split_axis=0, concat_axis=2, tiled=True)
     width = shared.shape[2]
     columns = shared.reshape(shared.shape[0], shared.shape[1], width * 2)

time: 566 us -> 636 us (1.12)
  blocking collectives: 0 us -> 193 us
  waiting for transfers between devices: 295 us -> 184 us
  between operations: 13.8 us -> 0.42 us
    all_to_all x0 -> x1, blocking collectives: none -> 193 us  [lax.all_to_all(jnp.stack([packet] * lax.axis_size(shard_axis), 0), shard_...]
    all_gather x1 -> x0, waiting for transfers between devices: 111 us -> none  [shards(): gathered = lax.all_gather(spectra, 'az', axis=1, tiled=True)]
    reshape x0 -> x1, local copies, waits for them, and re-layouts: none -> 26 us  [jnp.concatenate(lax.all_to_all(jnp.stack([packet] * lax.axis_size(shard_a...]
    all_gather x1 -> x0, local copies, waits for them, and re-layouts: 26 us -> none  [shards(): gathered = lax.all_gather(spectra, 'az', axis=1, tiled=True)]
  transfers between devices with their start and end apart: 4 -> 3, of which waited for: 2 -> 1; matrix products, arithmetic and copies ran while one was open for 15% -> 13% of each run, Pallas kernels for 0% -> 0%
where the time goes in v1:
time: 636 us; the launch traced here: 632 us
  blocking collectives  193 us (30%)
  waiting for transfers between devices  184 us (29%)
  local copies, waits for them, and re-layouts  151 us (24%)
  other arithmetic  60.8 us (10%)
  matrix products  34.4 us (5%)
  starting transfers between devices  8.77 us (1%)
    all_to_all x1, blocking collectives, lax.all_to_all(jnp.stack([packet] * lax.axis_size(shard_axis), 0), shard_...  193 us
    all_to_all x1, waiting for transfers between devices, shards(): lax.all_to_all(gathered, 'tm', split_axis=0, concat_axis=2, tiled=True)  184 us
    unnamed x15, local copies, waits for them, and re-layouts  58 us
    convert_element_type x1, other arithmetic, shards(): total.astype(jnp.bfloat16).reshape(cycles * sector * blocks, length)  26 us
    reshape x1, local copies, waits for them, and re-layouts, jnp.concatenate(lax.all_to_all(jnp.stack([packet] * lax.axis_size(shard_a...  26 us
    reshape x1, local copies, waits for them, and re-layouts, shards(): columns = shared.reshape(shared.shape[0], shared.shape[1], width * 2)  23.2 us
    another operation x1, other arithmetic  19.2 us
    all_to_all x1, local copies, waits for them, and re-layouts, shards(): lax.all_to_all(gathered, 'tm', split_axis=0, concat_axis=2, tiled=True)  18.6 us
  transfers between devices with their start and end apart: 3, of which 1 were waited for; matrix products, arithmetic and copies ran while one was open for 13% of the time, Pallas kernels for 0%

profile of v1, /device:TPU:1, one launch (start us, length us, event | category | flops | bytes accessed | tf_op | source)
XLA Modules:
  0.0 632.0 jit_solution(5746003530437398540)
XLA Ops:
  0.0 0.0 copy-start
  0.0 0.0 copy-start.1
  0.0 4.7 fusion.19
  4.7 3.0 collective-permute-start
  7.8 0.0 collective-permute-start.1
  7.8 0.0 copy-done
  7.8 0.0 copy-done.1
  7.8 2.1 mul.142
  9.9 19.6 %copy.35 = f32[128,8,16,256]{3,1,2,0:T(8,128)} copy(f32[128,8,16,256]{3,2,1,0:T(8,128)S(1)} %bitcast.41) | data formatting | bytes 33554432
  29.5 2.1 mul.137
  31.7 19.0 %copy.34 = f32[128,8,16,256]{3,1,2,0:T(8,128)} copy(f32[128,8,16,256]{3,2,1,0:T(8,128)S(1)} %bitcast.42) | data formatting | bytes 33554432
  50.7 2.1 mul.132
  52.9 0.0 slice-start
  52.9 0.0 slice-start.1
  52.9 19.3 %copy.33 = f32[128,8,16,256]{3,1,2,0:T(8,128)} copy(f32[128,8,16,256]{3,2,1,0:T(8,128)S(1)} %bitcast.43) | data formatting | bytes 33554432
  72.2 0.1 subtract_multiply_fusion
  72.3 0.0 slice-start.2
  72.3 19.2 %multiply_convert_fusion.1 = (bf16[4096,256]{1,0:T(8,128)(2,1)}, bf16[4096,256]{1,0:T(8,128)(2,1)}) fusion(s32[256]{0:T(256)S(1)} %iota_add_fusion, f32[4096]{0:T(1024)S(1)} %get-tuple-element.16, f32[4096]{0:T(1024)S(1)} %get-tuple-element.17), kind=kLoop, calls=%fused_computation.20 | loop fusion | flops 18874368 | bytes 4228096 | tf_op jit(solution)/shard_map/convert.3
  91.5 0.0 slice-start.3
  91.5 0.0 collective-permute-done
  91.5 0.0 collective-permute-done.1
  91.5 0.0 slice-done
  91.5 0.0 slice-done.1
  91.5 8.1 %pad_maximum_fusion.1 = (bf16[16,4,16,4096]{3,2,1,0:T(8,128)(2,1)}, bf16[16,4,16,4096]{3,2,1,0:T(8,128)(2,1)}) fusion(bf16[16,4,16,4096]{3,2,1,0:T(8,128)(2,1)S(1)} %bitcast.47, bf16[16,1,16,4096]{3,2,1,0:T(8,128)(2,1)} %collective-permute-done, bf16[16,1,16,4096]{3,2,1,0:T(8,128)(2,1)} %collective-permute-done.1), kind=kLoop, calls=%fused_computation.8 | loop fusion | flops 8388608 | bytes 29360128 | tf_op jit(solution)/shard_map/concatenate | solution.py:23
  99.6 0.0 slice-done.2
  99.7 0.0 slice-done.3
  99.7 26.0 %fusion.1 = bf16[1024,4096]{1,0:T(8,128)(2,1)} fusion(f32[1024,4096]{1,0:T(8,128)} %bitcast.38, f32[1024,4096]{1,0:T(8,128)} %bitcast.39, f32[1024,4096]{1,0:T(8,128)} %bitcast.40, bf16[16,4,16,4096]{3,2,1,0:T(8,128)(2,1)} %get-tuple-element.6, bf16[16,4,16,4096]{3,2,1,0:T(8,128)(2,1)S(1)} %bitcast.49, bf16[16,4,16,4096]{3,2,1,0:T(8,128)(2,1)} %get-tuple-element.5), kind=kLoop, calls=%fused_computation.3 | loop fusion | flops 37748736 | bytes 83886080 | tf_op jit(solution)/shard_map/convert_element_type | solution.py:68
  125.7 9.1 %fusion.14 = bf16[1024,512]{1,0:T(8,128)(2,1)S(1)} fusion(bf16[1024,4096]{1,0:T(8,128)(2,1)} %fusion.1, bf16[4096,256]{1,0:T(8,128)(2,1)} %get-tuple-element.15, bf16[4096,256]{1,0:T(8,128)(2,1)} %get-tuple-element.14), kind=kOutput, calls=%fused_computation.28 | convolution fusion | flops 4303880192 | bytes 13631488 | tf_op jit(solution)/shard_map/dot_general | solution.py:71
  134.7 0.5 reshape.58
  135.2 0.2 copy.24
  135.4 2.2 stack.16
  137.6 193.3 %all_to_all.20 = bf16[16,256,64,16,2]{1,3,4,2,0:T(8,128)(2,1)} all-to-all(bf16[16,256,64,16,2]{1,3,4,2,0:T(8,128)(2,1)S(1)} %stack.16), channel_id=1, replica_groups=mesh['az'=16,'tm'=8] {'az'}, dimensions={0} | all-to-all | bytes 33554432 | tf_op jit(solution)/shard_map/all_to_all | solution.py:9
  331.0 26.0 %copy.25 = bf16[256,1024,16,2]{1,2,3,0:T(8,128)(2,1)} copy(bf16[256,1024,16,2]{0,2,3,1:T(8,128)(2,1)} %bitcast.44) | data formatting | bytes 33554432 | tf_op jit(solution)/shard_map/reshape | solution.py:8
  356.9 5.8 all-to-all-start.1
  362.7 183.7 %all-to-all-done.1 = bf16[256,1024,16,2]{1,2,3,0:T(8,128)(2,1)} async-done(((bf16[256,1024,16,2]{1,2,3,0:T(8,128)(2,1)}), bf16[256,1024,16,2]{1,2,3,0:T(8,128)(2,1)}, u32[]{:S(2)}, u32[]{:S(2)}) %all-to-all-start.1) | async-done | bytes 16777248 | tf_op jit(solution)/shard_map/all_to_all | solution.py:76
  546.4 18.6 %copy.26 = bf16[32,1024,8,16,2]{1,0,4,3,2:T(8,128)(2,1)} copy(bf16[32,1024,8,16,2]{1,3,4,0,2:T(8,128)(2,1)} %bitcast.8) | data formatting | bytes 33554432 | tf_op jit(solution)/shard_map/all_to_all | solution.py:76
  565.1 23.2 %copy.27 = bf16[32,1024,256]{2,1,0:T(8,128)(2,1)} copy(bf16[32,1024,256]{1,0,2:T(8,128)(2,1)} %bitcast.45) | data formatting | bytes 33554432 | tf_op jit(solution)/shard_map/reshape | solution.py:78
  588.3 1.3 constant_dynamic-slice_fusion
  589.6 3.1 copy.29
  592.7 14.1 %convolution_bitcast_fusion = f32[32,1,64,1024]{3,2,0,1:T(8,128)} fusion(bf16[32,64,256]{2,1,0:T(8,128)(2,1)S(1)} %constant_dynamic-slice_fusion, bf16[32,1024,256]{2,1,0:T(8,128)(2,1)} %copy.27), kind=kOutput, calls=%fused_computation.24 | convolution fusion | flops 1073741824 | bytes 26214400 | tf_op jit(solution)/shard_map/fqk,fpk->fqp/dot_general | solution.py:53
  606.8 0.2 fusion.20
  607.1 0.4 pad_maximum_fusion.2
  607.5 11.2 %convolution_bitcast_fusion.1 = f32[32,1,64,1024]{3,2,0,1:T(8,128)} fusion(bf16[32,1024,256]{2,1,0:T(8,128)(2,1)} %copy.27, bf16[32,64,256]{1,0,2:T(8,128)(2,1)S(1)} %bitcast.50), kind=kOutput, calls=%fused_computation.25 | convolution fusion | flops 1073741824 | bytes 26214400 | tf_op jit(solution)/shard_map/fqk,fpk->fqp/dot_general | solution.py:54
  618.7 6.8 %maximum_multiply_fusion = f32[32,2,64,1024]{3,2,0,1:T(8,128)S(1)} fusion(f32[32,1,64,1024]{3,2,0,1:T(8,128)} %convolution_bitcast_fusion.1, f32[32,1,64,1024]{3,2,0,1:T(8,128)} %convolution_bitcast_fusion), kind=kLoop, calls=%fused_computation | loop fusion | flops 8388608 | bytes 33554432 | tf_op jit(solution)/shard_map/mul | solution.py:82
  625.6 6.2 copy.32
  (4 shorter events, 0.0 us)
Async XLA Ops:
  0.0 7.8 %copy-start = (f32[16,16]{1,0:T(8,128)S(1)}, f32[16,16]{1,0:T(8,128)}, u32[]{:S(2)}) copy-start(f32[16,16]{1,0:T(8,128)} %param.5) | copy-start | bytes 3076
  0.0 7.8 %copy-start.1 = (s32[16,16]{1,0:T(8,128)S(1)}, s32[16,16]{1,0:T(8,128)}, u32[]{:S(2)}) copy-start(s32[16,16]{1,0:T(8,128)} %param.4) | copy-start | bytes 3076
  4.7 86.8 %collective-permute-start = (bf16[16,1,16,4096]{3,2,1,0:T(8,128)(2,1)}, bf16[16,1,16,4096]{3,2,1,0:T(8,128)(2,1)}, u32[]{:S(2)}, u32[]{:S(2)}) collective-permute-start(bf16[16,1,16,4096]{3,2,1,0:T(8,128)(2,1)} %get-tuple-element.7), channel_id=1, source_target_pairs={{0,8},{8,16},{16,24},{24,32},{32,40},{40,48},{48,56},{56,64},{64,7... | collective-permute-start | bytes 6291464 | tf_op jit(solution)/shard_map/ppermute | solution.py:19
  7.8 83.8 %collective-permute-start.1 = (bf16[16,1,16,4096]{3,2,1,0:T(8,128)(2,1)}, bf16[16,1,16,4096]{3,2,1,0:T(8,128)(2,1)}, u32[]{:S(2)}, u32[]{:S(2)}) collective-permute-start(bf16[16,1,16,4096]{3,2,1,0:T(8,128)(2,1)} %get-tuple-element.8), channel_id=1, source_target_pairs={{8,0},{16,8},{24,16},{32,24},{40,32},{48,40},{56,48},{64,56},{72,6... | collective-permute-start | bytes 6291464 | tf_op jit(solution)/shard_map/ppermute | solution.py:22
  52.9 38.7 %slice-start = ((s8[8388608]{0:T(1024)(128)(4,1)}), s8[4194304]{0:T(1024)(128)(4,1)S(1)}, s32[]{:S(2)}) async-start(s8[8388608]{0:T(1024)(128)(4,1)} %bitcast.46), calls=%async_computation.2 | async-start | bytes 8388608
  52.9 38.7 %slice-start.1 = ((s8[8388608]{0:T(1024)(128)(4,1)}), s8[4194304]{0:T(1024)(128)(4,1)S(1)}, s32[]{:S(2)}) async-start(s8[8388608]{0:T(1024)(128)(4,1)} %bitcast.46), calls=%async_computation.3 | async-start | bytes 8388608
  72.3 27.4 %slice-start.2 = ((s8[8388608]{0:T(1024)(128)(4,1)}), s8[4194304]{0:T(1024)(128)(4,1)S(1)}, s32[]{:S(2)}) async-start(s8[8388608]{0:T(1024)(128)(4,1)} %bitcast.48), calls=%async_computation.4 | async-start | bytes 8388608
  91.5 8.2 %slice-start.3 = ((s8[8388608]{0:T(1024)(128)(4,1)}), s8[4194304]{0:T(1024)(128)(4,1)S(1)}, s32[]{:S(2)}) async-start(s8[8388608]{0:T(1024)(128)(4,1)} %bitcast.48), calls=%async_computation.5 | async-start | bytes 8388608
  356.9 189.5 %all-to-all-start.1 = ((bf16[256,1024,16,2]{1,2,3,0:T(8,128)(2,1)}), bf16[256,1024,16,2]{1,2,3,0:T(8,128)(2,1)}, u32[]{:S(2)}, u32[]{:S(2)}) async-start(bf16[256,1024,16,2]{1,2,3,0:T(8,128)(2,1)} %copy.25), calls=%async_computation.1 | async-start | bytes 33554432 | tf_op jit(solution)/shard_map/all_to_all | solution.py:76
